TPU v7x, 32 devices: a whole 2x2x4 slice. The times are simulated.
32 devices in a mesh: section: 4 (over x, core), expert: 8 (over z, y).
Axes of the slice: x: 2, y: 2, z: 4, core: 2. Of those that a mesh axis runs over, the one named last changes fastest.
Arguments:
- layer_inputs: bfloat16 [4, 8, 128, 2048], P('section', None, 'expert'), may hold values from -6 to 6
- top_grad: bfloat16 [8, 128, 2048], P('section', 'expert'), may hold values from -6 to 6
- expert_ids: int32 [4, 8, 128, 4], P('section', None, 'expert'), may hold values from 0 to 7, all different within a row; in each aligned block of 16 rows (0 to 15, 16 to 31, ..., all dimensions but the last counted through in order) at most 9 rows name the same one
- router: bfloat16 [4, 2048, 8], P('section'), may hold values from -0.125 to 0.125
- norm_gain: bfloat16 [4, 2048], P('section'), may hold values from 0.099609375 to 1.8984375
- w_gate: bfloat16 [4, 8, 2048, 1024], P('section', 'expert'), may hold values from -0.125 to 0.125
- w_up: bfloat16 [4, 8, 2048, 1024], P('section', 'expert'), may hold values from -0.125 to 0.125
- w_down: bfloat16 [4, 8, 1024, 2048], P('section', 'expert'), may hold values from -0.1875 to 0.1875
Outputs:
- input_grads: bfloat16 [4, 8, 128, 2048], P('section', None, 'expert')
Inputs may be any that keep to these rules, and one draw needn't show every extreme that they name: `expert_ids`: each token names 4 different experts. Among the 16 tokens of one device in one micro-batch of one layer, no expert is named by more than 9 of them, and in some of these blocks one expert is named by exactly 9.
All inputs are finite; a program needn't handle non-finite values.
Results may differ from a plain program's by a relative error of at most 0.015.
Values may be sent and summed in bfloat16 or wider, within the bound.
No kernel may reach another device: no remote copies, remote signals or barrier semaphores. Data moves between devices by JAX's collectives and lax.ppermute only.
A program may use at most 128 MiB of HBM per device.

v0:
```python
import jax
import jax.numpy as jnp
from jax import lax
from jax.sharding import PartitionSpec as P


def shifted(shard, axis, by):
    devices = lax.axis_size(axis)
    pairs = [(i, i + by) for i in range(devices) if 0 <= i + by < devices]
    return lax.ppermute(shard, axis, pairs)


def prepare(x_rows, gain):
    x_float = x_rows.astype(jnp.float32)
    inverse = lax.rsqrt(jnp.mean(x_float * x_float, axis=-1, keepdims=True) + 1e-05)
    normed = (x_float * inverse * gain).astype(jnp.bfloat16)
    return (x_float, inverse, normed)


def expert_rows(normed_rows, grad_rows, gate_w, up_w, down_w):
    gate = jnp.dot(normed_rows, gate_w, preferred_element_type=jnp.float32)
    up_rows = jnp.dot(normed_rows, up_w, preferred_element_type=jnp.float32)
    squash = jax.nn.sigmoid(gate)
    active = gate * squash
    hidden = (active * up_rows).astype(jnp.bfloat16)
    output = jnp.dot(hidden, down_w, preferred_element_type=jnp.float32)
    dprob = jnp.sum(output * grad_rows.astype(jnp.float32), axis=-1)
    dhidden = lax.dot_general(
        grad_rows, down_w, (((1,), (1,)), ((), ())), preferred_element_type=jnp.float32
    )
    dgate = (dhidden * up_rows * squash * (1.0 + gate * (1.0 - squash))).astype(jnp.bfloat16)
    dup = (dhidden * active).astype(jnp.bfloat16)
    returned = lax.dot_general(
        dgate, gate_w, (((1,), (1,)), ((), ())), preferred_element_type=jnp.float32
    )
    returned = returned + lax.dot_general(
        dup, up_w, (((1,), (1,)), ((), ())), preferred_element_type=jnp.float32
    )
    return (returned.astype(jnp.bfloat16), dprob)


def finish(x_float, inverse, normed, gain, router_layer, ids, grad_in, pair_back, pair_prob):
    logits = jnp.dot(normed, router_layer, preferred_element_type=jnp.float32)
    raised = jnp.exp(logits)
    probs = raised / jnp.sum(raised, axis=-1, keepdims=True)
    choose = (ids[..., None] == jnp.arange(router_layer.shape[1], dtype=jnp.int32)).astype(
        jnp.float32
    )
    picked = jnp.sum(probs[..., None, :] * choose, axis=-1)
    dfull = jnp.sum(pair_prob[..., None] * choose, axis=-2)
    dlogit = probs * (dfull - jnp.sum(probs * dfull, axis=-1, keepdims=True))
    router_term = jnp.dot(
        dlogit, router_layer.astype(jnp.float32).T, precision=lax.Precision.HIGHEST
    )
    dnormed = jnp.sum(picked[..., None] * pair_back, axis=-2) + router_term
    scaled = gain * dnormed
    inner = jnp.mean(x_float * scaled, axis=-1, keepdims=True)
    result = (
        grad_in.astype(jnp.float32)
        + inverse * scaled
        - x_float * inverse * inverse * inverse * inner
    )
    return result.astype(jnp.bfloat16)


def selection(ids, experts, capacity):
    pair_ids = ids.reshape(-1)
    onehot = (pair_ids[:, None] == jnp.arange(experts, dtype=jnp.int32)[None, :]).astype(jnp.int32)
    ranks = jnp.sum(onehot * (jnp.cumsum(onehot, axis=0) - 1), axis=1)
    target = pair_ids * capacity + ranks
    return (target[:, None] == jnp.arange(experts * capacity, dtype=jnp.int32)[None, :]).astype(
        jnp.bfloat16
    )


def pack_rows(select, rows, per_token):
    repeated = jnp.repeat(rows, per_token, axis=0)
    packed = lax.dot_general(
        select, repeated, (((0,), (0,)), ((), ())), preferred_element_type=jnp.float32
    )
    return packed.astype(jnp.bfloat16)


def pick_micro(values, index):
    return lax.dynamic_index_in_dim(values, index, 0, False)


def shards(layer_inputs, top_grad, expert_ids, router, norm_gain, w_gate, w_up, w_down):
    segments = lax.axis_size("section")
    experts = lax.axis_size("expert")
    segment_index = lax.axis_index("section")
    micro = layer_inputs.shape[1]
    tok_rows = layer_inputs.shape[2]
    width = layer_inputs.shape[3]
    per_token = expert_ids.shape[3]
    capacity = min(tok_rows, per_token * tok_rows // experts + max(1, tok_rows // 16))
    slots = experts * capacity
    gain = norm_gain[0].astype(jnp.float32)
    router_layer = router[0]
    gate_layer = w_gate[0, 0]
    up_layer = w_up[0, 0]
    down_layer = w_down[0, 0]
    ids_layer = expert_ids[0]
    x_layer = layer_inputs[0]
    top_full = lax.all_gather(top_grad, "section", axis=0, tiled=True)

    def advance(step, carry):
        previous, collected = carry
        arrived = shifted(previous, "section", -1)
        position = step - (segments - 1 - segment_index)
        working = jnp.logical_and(position >= 0, position < micro)
        chosen = jnp.clip(position, 0, micro - 1)
        grad_in = jnp.where(segment_index == segments - 1, pick_micro(top_full, chosen), arrived)
        ids_now = pick_micro(ids_layer, chosen)
        select = selection(ids_now, experts, capacity)
        x_float, inverse, normed = prepare(pick_micro(x_layer, chosen), gain)
        sent_normed = pack_rows(select, normed, per_token).reshape(experts, capacity, width)
        sent_grad = pack_rows(select, grad_in, per_token).reshape(experts, capacity, width)
        got_normed, got_grad = (
            lax.all_to_all(sent_normed, "expert", split_axis=0, concat_axis=0, tiled=True),
            lax.all_to_all(sent_grad, "expert", split_axis=0, concat_axis=0, tiled=True),
        )
        rows_normed = got_normed.reshape(slots, width)
        rows_grad = got_grad.reshape(slots, width)

        def run_expert(operands):
            return expert_rows(operands[0], operands[1], gate_layer, up_layer, down_layer)

        def skip_expert(operands):
            return (jnp.zeros((slots, width), jnp.bfloat16), jnp.zeros((slots,), jnp.float32))

        returned, dprob = lax.cond(working, run_expert, skip_expert, (rows_normed, rows_grad))
        back_home, prob_home = (
            lax.all_to_all(
                returned.reshape(experts, capacity, width),
                "expert",
                split_axis=0,
                concat_axis=0,
                tiled=True,
            ),
            lax.all_to_all(
                dprob.reshape(experts, capacity).astype(jnp.bfloat16),
                "expert",
                split_axis=0,
                concat_axis=0,
                tiled=True,
            ).astype(jnp.float32),
        )
        pair_back = lax.dot_general(
            select,
            back_home.reshape(slots, width),
            (((1,), (0,)), ((), ())),
            preferred_element_type=jnp.float32,
        )
        pair_back = pair_back.reshape(tok_rows, per_token, width)
        pair_prob = jnp.dot(
            select.astype(jnp.float32), prob_home.reshape(slots), precision=lax.Precision.HIGHEST
        )
        pair_prob = pair_prob.reshape(tok_rows, per_token)
        result = finish(
            x_float, inverse, normed, gain, router_layer, ids_now, grad_in, pair_back, pair_prob
        )
        retained = pick_micro(collected, chosen)
        collected = lax.dynamic_update_index_in_dim(
            collected, jnp.where(working, result, retained), chosen, 0
        )
        return (result, collected)

    start = (
        jnp.zeros((tok_rows, width), jnp.bfloat16),
        jnp.zeros((micro, tok_rows, width), jnp.bfloat16),
    )
    final_grad, collected = lax.fori_loop(0, micro + segments - 1, advance, start)
    return collected.reshape(1, micro, tok_rows, width)


def solution(mesh):
    placed = (
        P("section", None, "expert", None),
        P("section", "expert", None),
        P("section", None, "expert", None),
        P("section", None, None),
        P("section", None),
        P("section", "expert", None, None),
        P("section", "expert", None, None),
        P("section", "expert", None, None),
    )
    return jax.shard_map(
        shards,
        mesh=mesh,
        in_specs=placed,
        out_specs=P("section", None, "expert", None),
        check_vma=False,
    )
```

profile of v0, /device:TPU:2, one launch (start us, length us, event | category | flops | bytes accessed | tf_op | source)
XLA Modules:
  0.0 932.1 jit_solution(10642153080023947241)
XLA Ops:
  9.2 922.1 %while.18 = (s32[]{:T(128)}, bf16[16,2048]{1,0:T(8,128)(2,1)S(1)}, bf16[8,16,2048]{2,1,0:T(8,128)(2,1)S(1)}, pred[]{:T(512)}, s32[]{:T(128)}, /*index=5*/bf16[8,...) while((s32[]{:T(128)}, bf16[16,2048]{1,0:T(8,128)(2,1)S(1)}, ...), condition=%wide.region_13.14_spmd.clone, body=%wide.region_0.13_spmd.clone.sunk | while | flops 1876001664 | bytes 93928576 | solution.py:173
  40.5 14.4 %all-to-all-done = bf16[8,9,2048]{2,1,0:T(8,128)(2,1)S(1)} async-done(((bf16[8,9,2048]{2,1,0:T(8,128)(2,1)}), bf16[8,9,2048]{2,1,0:T(8,128)(2,1)S(1)}, u32[]{:S(2)}, u32[]{:S(2)}) %all-to-all-start) | async-done | bytes 294944 | tf_op jit(solution)/shard_map/while/body/eval_jaxpr/all_to_all | solution.py:121
  120.1 14.1 %conditional.3 = (bf16[72,2048]{1,0:T(8,128)(2,1)S(1)}, bf16[72]{0:T(256)(128)(2,1)S(1)}) conditional(s32[]{:T(128)} %convert_element_type.180, () %tuple.64, (bf16[8,9,2048]{2,1,0:T(8,128)(2,1)S(1)}, bf16[1024,2048]{1,0:T(8,128)(2,1)}, bf16[8,9,2048]{2,1,0:T(8,128)(2,1)S(1)}, bf16[2048,1024]{1,0:T(8,128)(2,1)}, bf16[2048,1024]{1,0:T(8,128)(2,1)}) %tuple.65), branch_computations={%region_6.6_spmd, %region_7.8_spmd} | conditional | flops 1814298624 | bytes 82280696 | solution.py:132
  151.3 14.9 %all-to-all-done.2 = bf16[8,9,2048]{2,1,0:T(8,128)(2,1)S(1)} async-done(((bf16[8,9,2048]{2,1,0:T(8,128)(2,1)}), bf16[8,9,2048]{2,1,0:T(8,128)(2,1)S(1)}, u32[]{:S(2)}, u32[]{:S(2)}) %all-to-all-start.2) | async-done | bytes 294944 | tf_op jit(solution)/shard_map/while/body/eval_jaxpr/all_to_all | solution.py:134
  180.9 13.7 %all-to-all-done.1 = bf16[8,9,2048]{2,1,0:T(8,128)(2,1)S(1)} async-done(((bf16[8,9,2048]{2,1,0:T(8,128)(2,1)}), bf16[8,9,2048]{2,1,0:T(8,128)(2,1)S(1)}, u32[]{:S(2)}, u32[]{:S(2)}) %all-to-all-start.1) | async-done | bytes 294944 | tf_op jit(solution)/shard_map/while/body/eval_jaxpr/all_to_all | solution.py:120
  198.4 14.5 %all-to-all-done = bf16[8,9,2048]{2,1,0:T(8,128)(2,1)S(1)} async-done(((bf16[8,9,2048]{2,1,0:T(8,128)(2,1)}), bf16[8,9,2048]{2,1,0:T(8,128)(2,1)S(1)}, u32[]{:S(2)}, u32[]{:S(2)}) %all-to-all-start) | async-done | bytes 294944 | tf_op jit(solution)/shard_map/while/body/eval_jaxpr/all_to_all | solution.py:121
  212.9 14.1 %conditional.3 = (bf16[72,2048]{1,0:T(8,128)(2,1)S(1)}, bf16[72]{0:T(256)(128)(2,1)S(1)}) conditional(s32[]{:T(128)} %convert_element_type.180, () %tuple.64, (bf16[8,9,2048]{2,1,0:T(8,128)(2,1)S(1)}, bf16[1024,2048]{1,0:T(8,128)(2,1)}, bf16[8,9,2048]{2,1,0:T(8,128)(2,1)S(1)}, bf16[2048,1024]{1,0:T(8,128)(2,1)}, bf16[2048,1024]{1,0:T(8,128)(2,1)}) %tuple.65), branch_computations={%region_6.6_spmd, %region_7.8_spmd} | conditional | flops 1814298624 | bytes 82280696 | solution.py:132
  269.0 13.7 %all-to-all-done.1 = bf16[8,9,2048]{2,1,0:T(8,128)(2,1)S(1)} async-done(((bf16[8,9,2048]{2,1,0:T(8,128)(2,1)}), bf16[8,9,2048]{2,1,0:T(8,128)(2,1)S(1)}, u32[]{:S(2)}, u32[]{:S(2)}) %all-to-all-start.1) | async-done | bytes 294944 | tf_op jit(solution)/shard_map/while/body/eval_jaxpr/all_to_all | solution.py:120
  286.6 14.5 %all-to-all-done = bf16[8,9,2048]{2,1,0:T(8,128)(2,1)S(1)} async-done(((bf16[8,9,2048]{2,1,0:T(8,128)(2,1)}), bf16[8,9,2048]{2,1,0:T(8,128)(2,1)S(1)}, u32[]{:S(2)}, u32[]{:S(2)}) %all-to-all-start) | async-done | bytes 294944 | tf_op jit(solution)/shard_map/while/body/eval_jaxpr/all_to_all | solution.py:121
  301.1 14.1 %conditional.3 = (bf16[72,2048]{1,0:T(8,128)(2,1)S(1)}, bf16[72]{0:T(256)(128)(2,1)S(1)}) conditional(s32[]{:T(128)} %convert_element_type.180, () %tuple.64, (bf16[8,9,2048]{2,1,0:T(8,128)(2,1)S(1)}, bf16[1024,2048]{1,0:T(8,128)(2,1)}, bf16[8,9,2048]{2,1,0:T(8,128)(2,1)S(1)}, bf16[2048,1024]{1,0:T(8,128)(2,1)}, bf16[2048,1024]{1,0:T(8,128)(2,1)}) %tuple.65), branch_computations={%region_6.6_spmd, %region_7.8_spmd} | conditional | flops 1814298624 | bytes 82280696 | solution.py:132
  329.9 13.0 %all-to-all-done.2 = bf16[8,9,2048]{2,1,0:T(8,128)(2,1)S(1)} async-done(((bf16[8,9,2048]{2,1,0:T(8,128)(2,1)}), bf16[8,9,2048]{2,1,0:T(8,128)(2,1)S(1)}, u32[]{:S(2)}, u32[]{:S(2)}) %all-to-all-start.2) | async-done | bytes 294944 | tf_op jit(solution)/shard_map/while/body/eval_jaxpr/all_to_all | solution.py:134
  357.2 13.7 %all-to-all-done.1 = bf16[8,9,2048]{2,1,0:T(8,128)(2,1)S(1)} async-done(((bf16[8,9,2048]{2,1,0:T(8,128)(2,1)}), bf16[8,9,2048]{2,1,0:T(8,128)(2,1)S(1)}, u32[]{:S(2)}, u32[]{:S(2)}) %all-to-all-start.1) | async-done | bytes 294944 | tf_op jit(solution)/shard_map/while/body/eval_jaxpr/all_to_all | solution.py:120
  374.7 14.5 %all-to-all-done = bf16[8,9,2048]{2,1,0:T(8,128)(2,1)S(1)} async-done(((bf16[8,9,2048]{2,1,0:T(8,128)(2,1)}), bf16[8,9,2048]{2,1,0:T(8,128)(2,1)S(1)}, u32[]{:S(2)}, u32[]{:S(2)}) %all-to-all-start) | async-done | bytes 294944 | tf_op jit(solution)/shard_map/while/body/eval_jaxpr/all_to_all | solution.py:121
  389.2 14.1 %conditional.3 = (bf16[72,2048]{1,0:T(8,128)(2,1)S(1)}, bf16[72]{0:T(256)(128)(2,1)S(1)}) conditional(s32[]{:T(128)} %convert_element_type.180, () %tuple.64, (bf16[8,9,2048]{2,1,0:T(8,128)(2,1)S(1)}, bf16[1024,2048]{1,0:T(8,128)(2,1)}, bf16[8,9,2048]{2,1,0:T(8,128)(2,1)S(1)}, bf16[2048,1024]{1,0:T(8,128)(2,1)}, bf16[2048,1024]{1,0:T(8,128)(2,1)}) %tuple.65), branch_computations={%region_6.6_spmd, %region_7.8_spmd} | conditional | flops 1814298624 | bytes 82280696 | solution.py:132
  445.4 13.7 %all-to-all-done.1 = bf16[8,9,2048]{2,1,0:T(8,128)(2,1)S(1)} async-done(((bf16[8,9,2048]{2,1,0:T(8,128)(2,1)}), bf16[8,9,2048]{2,1,0:T(8,128)(2,1)S(1)}, u32[]{:S(2)}, u32[]{:S(2)}) %all-to-all-start.1) | async-done | bytes 294944 | tf_op jit(solution)/shard_map/while/body/eval_jaxpr/all_to_all | solution.py:120
  462.9 14.5 %all-to-all-done = bf16[8,9,2048]{2,1,0:T(8,128)(2,1)S(1)} async-done(((bf16[8,9,2048]{2,1,0:T(8,128)(2,1)}), bf16[8,9,2048]{2,1,0:T(8,128)(2,1)S(1)}, u32[]{:S(2)}, u32[]{:S(2)}) %all-to-all-start) | async-done | bytes 294944 | tf_op jit(solution)/shard_map/while/body/eval_jaxpr/all_to_all | solution.py:121
  477.4 14.1 %conditional.3 = (bf16[72,2048]{1,0:T(8,128)(2,1)S(1)}, bf16[72]{0:T(256)(128)(2,1)S(1)}) conditional(s32[]{:T(128)} %convert_element_type.180, () %tuple.64, (bf16[8,9,2048]{2,1,0:T(8,128)(2,1)S(1)}, bf16[1024,2048]{1,0:T(8,128)(2,1)}, bf16[8,9,2048]{2,1,0:T(8,128)(2,1)S(1)}, bf16[2048,1024]{1,0:T(8,128)(2,1)}, bf16[2048,1024]{1,0:T(8,128)(2,1)}) %tuple.65), branch_computations={%region_6.6_spmd, %region_7.8_spmd} | conditional | flops 1814298624 | bytes 82280696 | solution.py:132
  533.5 13.7 %all-to-all-done.1 = bf16[8,9,2048]{2,1,0:T(8,128)(2,1)S(1)} async-done(((bf16[8,9,2048]{2,1,0:T(8,128)(2,1)}), bf16[8,9,2048]{2,1,0:T(8,128)(2,1)S(1)}, u32[]{:S(2)}, u32[]{:S(2)}) %all-to-all-start.1) | async-done | bytes 294944 | tf_op jit(solution)/shard_map/while/body/eval_jaxpr/all_to_all | solution.py:120
  551.0 14.5 %all-to-all-done = bf16[8,9,2048]{2,1,0:T(8,128)(2,1)S(1)} async-done(((bf16[8,9,2048]{2,1,0:T(8,128)(2,1)}), bf16[8,9,2048]{2,1,0:T(8,128)(2,1)S(1)}, u32[]{:S(2)}, u32[]{:S(2)}) %all-to-all-start) | async-done | bytes 294944 | tf_op jit(solution)/shard_map/while/body/eval_jaxpr/all_to_all | solution.py:121
  565.5 14.1 %conditional.3 = (bf16[72,2048]{1,0:T(8,128)(2,1)S(1)}, bf16[72]{0:T(256)(128)(2,1)S(1)}) conditional(s32[]{:T(128)} %convert_element_type.180, () %tuple.64, (bf16[8,9,2048]{2,1,0:T(8,128)(2,1)S(1)}, bf16[1024,2048]{1,0:T(8,128)(2,1)}, bf16[8,9,2048]{2,1,0:T(8,128)(2,1)S(1)}, bf16[2048,1024]{1,0:T(8,128)(2,1)}, bf16[2048,1024]{1,0:T(8,128)(2,1)}) %tuple.65), branch_computations={%region_6.6_spmd, %region_7.8_spmd} | conditional | flops 1814298624 | bytes 82280696 | solution.py:132
  621.7 13.7 %all-to-all-done.1 = bf16[8,9,2048]{2,1,0:T(8,128)(2,1)S(1)} async-done(((bf16[8,9,2048]{2,1,0:T(8,128)(2,1)}), bf16[8,9,2048]{2,1,0:T(8,128)(2,1)S(1)}, u32[]{:S(2)}, u32[]{:S(2)}) %all-to-all-start.1) | async-done | bytes 294944 | tf_op jit(solution)/shard_map/while/body/eval_jaxpr/all_to_all | solution.py:120
  639.2 14.5 %all-to-all-done = bf16[8,9,2048]{2,1,0:T(8,128)(2,1)S(1)} async-done(((bf16[8,9,2048]{2,1,0:T(8,128)(2,1)}), bf16[8,9,2048]{2,1,0:T(8,128)(2,1)S(1)}, u32[]{:S(2)}, u32[]{:S(2)}) %all-to-all-start) | async-done | bytes 294944 | tf_op jit(solution)/shard_map/while/body/eval_jaxpr/all_to_all | solution.py:121
  653.7 14.1 %conditional.3 = (bf16[72,2048]{1,0:T(8,128)(2,1)S(1)}, bf16[72]{0:T(256)(128)(2,1)S(1)}) conditional(s32[]{:T(128)} %convert_element_type.180, () %tuple.64, (bf16[8,9,2048]{2,1,0:T(8,128)(2,1)S(1)}, bf16[1024,2048]{1,0:T(8,128)(2,1)}, bf16[8,9,2048]{2,1,0:T(8,128)(2,1)S(1)}, bf16[2048,1024]{1,0:T(8,128)(2,1)}, bf16[2048,1024]{1,0:T(8,128)(2,1)}) %tuple.65), branch_computations={%region_6.6_spmd, %region_7.8_spmd} | conditional | flops 1814298624 | bytes 82280696 | solution.py:132
  709.8 13.7 %all-to-all-done.1 = bf16[8,9,2048]{2,1,0:T(8,128)(2,1)S(1)} async-done(((bf16[8,9,2048]{2,1,0:T(8,128)(2,1)}), bf16[8,9,2048]{2,1,0:T(8,128)(2,1)S(1)}, u32[]{:S(2)}, u32[]{:S(2)}) %all-to-all-start.1) | async-done | bytes 294944 | tf_op jit(solution)/shard_map/while/body/eval_jaxpr/all_to_all | solution.py:120
  727.4 14.5 %all-to-all-done = bf16[8,9,2048]{2,1,0:T(8,128)(2,1)S(1)} async-done(((bf16[8,9,2048]{2,1,0:T(8,128)(2,1)}), bf16[8,9,2048]{2,1,0:T(8,128)(2,1)S(1)}, u32[]{:S(2)}, u32[]{:S(2)}) %all-to-all-start) | async-done | bytes 294944 | tf_op jit(solution)/shard_map/while/body/eval_jaxpr/all_to_all | solution.py:121
  741.9 14.1 %conditional.3 = (bf16[72,2048]{1,0:T(8,128)(2,1)S(1)}, bf16[72]{0:T(256)(128)(2,1)S(1)}) conditional(s32[]{:T(128)} %convert_element_type.180, () %tuple.64, (bf16[8,9,2048]{2,1,0:T(8,128)(2,1)S(1)}, bf16[1024,2048]{1,0:T(8,128)(2,1)}, bf16[8,9,2048]{2,1,0:T(8,128)(2,1)S(1)}, bf16[2048,1024]{1,0:T(8,128)(2,1)}, bf16[2048,1024]{1,0:T(8,128)(2,1)}) %tuple.65), branch_computations={%region_6.6_spmd, %region_7.8_spmd} | conditional | flops 1814298624 | bytes 82280696 | solution.py:132
  794.8 13.7 %all-to-all-done.1 = bf16[8,9,2048]{2,1,0:T(8,128)(2,1)S(1)} async-done(((bf16[8,9,2048]{2,1,0:T(8,128)(2,1)}), bf16[8,9,2048]{2,1,0:T(8,128)(2,1)S(1)}, u32[]{:S(2)}, u32[]{:S(2)}) %all-to-all-start.1) | async-done | bytes 294944 | tf_op jit(solution)/shard_map/while/body/eval_jaxpr/all_to_all | solution.py:120
  812.3 14.5 %all-to-all-done = bf16[8,9,2048]{2,1,0:T(8,128)(2,1)S(1)} async-done(((bf16[8,9,2048]{2,1,0:T(8,128)(2,1)}), bf16[8,9,2048]{2,1,0:T(8,128)(2,1)S(1)}, u32[]{:S(2)}, u32[]{:S(2)}) %all-to-all-start) | async-done | bytes 294944 | tf_op jit(solution)/shard_map/while/body/eval_jaxpr/all_to_all | solution.py:121
  841.6 13.0 %all-to-all-done.2 = bf16[8,9,2048]{2,1,0:T(8,128)(2,1)S(1)} async-done(((bf16[8,9,2048]{2,1,0:T(8,128)(2,1)}), bf16[8,9,2048]{2,1,0:T(8,128)(2,1)S(1)}, u32[]{:S(2)}, u32[]{:S(2)}) %all-to-all-start.2) | async-done | bytes 294944 | tf_op jit(solution)/shard_map/while/body/eval_jaxpr/all_to_all | solution.py:134
  868.9 13.7 %all-to-all-done.1 = bf16[8,9,2048]{2,1,0:T(8,128)(2,1)S(1)} async-done(((bf16[8,9,2048]{2,1,0:T(8,128)(2,1)}), bf16[8,9,2048]{2,1,0:T(8,128)(2,1)S(1)}, u32[]{:S(2)}, u32[]{:S(2)}) %all-to-all-start.1) | async-done | bytes 294944 | tf_op jit(solution)/shard_map/while/body/eval_jaxpr/all_to_all | solution.py:120
  886.4 14.5 %all-to-all-done = bf16[8,9,2048]{2,1,0:T(8,128)(2,1)S(1)} async-done(((bf16[8,9,2048]{2,1,0:T(8,128)(2,1)}), bf16[8,9,2048]{2,1,0:T(8,128)(2,1)S(1)}, u32[]{:S(2)}, u32[]{:S(2)}) %all-to-all-start) | async-done | bytes 294944 | tf_op jit(solution)/shard_map/while/body/eval_jaxpr/all_to_all | solution.py:121
  915.6 13.0 %all-to-all-done.2 = bf16[8,9,2048]{2,1,0:T(8,128)(2,1)S(1)} async-done(((bf16[8,9,2048]{2,1,0:T(8,128)(2,1)}), bf16[8,9,2048]{2,1,0:T(8,128)(2,1)S(1)}, u32[]{:S(2)}, u32[]{:S(2)}) %all-to-all-start.2) | async-done | bytes 294944 | tf_op jit(solution)/shard_map/while/body/eval_jaxpr/all_to_all | solution.py:134
  (655 shorter events, 607.4 us)
Async XLA Ops:
  16.6 20.1 %all-to-all-start.1 = ((bf16[8,9,2048]{2,1,0:T(8,128)(2,1)}), bf16[8,9,2048]{2,1,0:T(8,128)(2,1)S(1)}, u32[]{:S(2)}, u32[]{:S(2)}) async-start(bf16[8,9,2048]{2,1,0:T(8,128)(2,1)} %reshape.265), calls=%async_computation.1 | async-start | bytes 1048576 | tf_op jit(solution)/shard_map/while/body/eval_jaxpr/all_to_all | solution.py:120
  36.7 18.2 %all-to-all-start = ((bf16[8,9,2048]{2,1,0:T(8,128)(2,1)}), bf16[8,9,2048]{2,1,0:T(8,128)(2,1)S(1)}, u32[]{:S(2)}, u32[]{:S(2)}) async-start(bf16[8,9,2048]{2,1,0:T(8,128)(2,1)} %reshape.263), calls=%async_computation | async-start | bytes 1048576 | tf_op jit(solution)/shard_map/while/body/eval_jaxpr/all_to_all | solution.py:121
  82.1 13.8 %collective-permute-start = (bf16[16,2048]{1,0:T(8,128)(2,1)S(1)}, bf16[16,2048]{1,0:T(8,128)(2,1)S(1)}, u32[]{:S(2)}, u32[]{:S(2)}) collective-permute-start(bf16[16,2048]{1,0:T(8,128)(2,1)S(1)} %broadcast_select_fusion.2), channel_id=1, source_target_pairs={{8,0},{16,8},{24,16},{9,1},{17,9},{25,17},{10,2},{18,10},{26,18},{... | collective-permute-start | bytes 196616 | tf_op jit(solution)/shard_map/while/body/eval_jaxpr/ppermute | solution.py:10
  91.1 14.7 %all-to-all-start.1 = ((bf16[8,9,2048]{2,1,0:T(8,128)(2,1)}), bf16[8,9,2048]{2,1,0:T(8,128)(2,1)S(1)}, u32[]{:S(2)}, u32[]{:S(2)}) async-start(bf16[8,9,2048]{2,1,0:T(8,128)(2,1)} %reshape.265), calls=%async_computation.1 | async-start | bytes 1048576 | tf_op jit(solution)/shard_map/while/body/eval_jaxpr/all_to_all | solution.py:120
  105.8 14.3 %all-to-all-start = ((bf16[8,9,2048]{2,1,0:T(8,128)(2,1)}), bf16[8,9,2048]{2,1,0:T(8,128)(2,1)S(1)}, u32[]{:S(2)}, u32[]{:S(2)}) async-start(bf16[8,9,2048]{2,1,0:T(8,128)(2,1)} %reshape.263), calls=%async_computation | async-start | bytes 1048576 | tf_op jit(solution)/shard_map/while/body/eval_jaxpr/all_to_all | solution.py:121
  147.4 18.9 %all-to-all-start.2 = ((bf16[8,9,2048]{2,1,0:T(8,128)(2,1)}), bf16[8,9,2048]{2,1,0:T(8,128)(2,1)S(1)}, u32[]{:S(2)}, u32[]{:S(2)}) async-start(bf16[8,9,2048]{2,1,0:T(8,128)(2,1)} %reshape.266), calls=%async_computation.2 | async-start | bytes 1048576 | tf_op jit(solution)/shard_map/while/body/eval_jaxpr/all_to_all | solution.py:134
  175.3 19.2 %all-to-all-start.1 = ((bf16[8,9,2048]{2,1,0:T(8,128)(2,1)}), bf16[8,9,2048]{2,1,0:T(8,128)(2,1)S(1)}, u32[]{:S(2)}, u32[]{:S(2)}) async-start(bf16[8,9,2048]{2,1,0:T(8,128)(2,1)} %reshape.265), calls=%async_computation.1 | async-start | bytes 1048576 | tf_op jit(solution)/shard_map/while/body/eval_jaxpr/all_to_all | solution.py:120
  194.6 18.3 %all-to-all-start = ((bf16[8,9,2048]{2,1,0:T(8,128)(2,1)}), bf16[8,9,2048]{2,1,0:T(8,128)(2,1)S(1)}, u32[]{:S(2)}, u32[]{:S(2)}) async-start(bf16[8,9,2048]{2,1,0:T(8,128)(2,1)} %reshape.263), calls=%async_computation | async-start | bytes 1048576 | tf_op jit(solution)/shard_map/while/body/eval_jaxpr/all_to_all | solution.py:121
  237.9 16.9 %all-to-all-start.2 = ((bf16[8,9,2048]{2,1,0:T(8,128)(2,1)}), bf16[8,9,2048]{2,1,0:T(8,128)(2,1)S(1)}, u32[]{:S(2)}, u32[]{:S(2)}) async-start(bf16[8,9,2048]{2,1,0:T(8,128)(2,1)} %reshape.266), calls=%async_computation.2 | async-start | bytes 1048576 | tf_op jit(solution)/shard_map/while/body/eval_jaxpr/all_to_all | solution.py:134
  263.9 18.8 %all-to-all-start.1 = ((bf16[8,9,2048]{2,1,0:T(8,128)(2,1)}), bf16[8,9,2048]{2,1,0:T(8,128)(2,1)S(1)}, u32[]{:S(2)}, u32[]{:S(2)}) async-start(bf16[8,9,2048]{2,1,0:T(8,128)(2,1)} %reshape.265), calls=%async_computation.1 | async-start | bytes 1048576 | tf_op jit(solution)/shard_map/while/body/eval_jaxpr/all_to_all | solution.py:120
  282.8 18.3 %all-to-all-start = ((bf16[8,9,2048]{2,1,0:T(8,128)(2,1)}), bf16[8,9,2048]{2,1,0:T(8,128)(2,1)S(1)}, u32[]{:S(2)}, u32[]{:S(2)}) async-start(bf16[8,9,2048]{2,1,0:T(8,128)(2,1)} %reshape.263), calls=%async_computation | async-start | bytes 1048576 | tf_op jit(solution)/shard_map/while/body/eval_jaxpr/all_to_all | solution.py:121
  326.0 16.9 %all-to-all-start.2 = ((bf16[8,9,2048]{2,1,0:T(8,128)(2,1)}), bf16[8,9,2048]{2,1,0:T(8,128)(2,1)S(1)}, u32[]{:S(2)}, u32[]{:S(2)}) async-start(bf16[8,9,2048]{2,1,0:T(8,128)(2,1)} %reshape.266), calls=%async_computation.2 | async-start | bytes 1048576 | tf_op jit(solution)/shard_map/while/body/eval_jaxpr/all_to_all | solution.py:134
  352.1 18.8 %all-to-all-start.1 = ((bf16[8,9,2048]{2,1,0:T(8,128)(2,1)}), bf16[8,9,2048]{2,1,0:T(8,128)(2,1)S(1)}, u32[]{:S(2)}, u32[]{:S(2)}) async-start(bf16[8,9,2048]{2,1,0:T(8,128)(2,1)} %reshape.265), calls=%async_computation.1 | async-start | bytes 1048576 | tf_op jit(solution)/shard_map/while/body/eval_jaxpr/all_to_all | solution.py:120
  370.9 18.3 %all-to-all-start = ((bf16[8,9,2048]{2,1,0:T(8,128)(2,1)}), bf16[8,9,2048]{2,1,0:T(8,128)(2,1)S(1)}, u32[]{:S(2)}, u32[]{:S(2)}) async-start(bf16[8,9,2048]{2,1,0:T(8,128)(2,1)} %reshape.263), calls=%async_computation | async-start | bytes 1048576 | tf_op jit(solution)/shard_map/while/body/eval_jaxpr/all_to_all | solution.py:121
  414.2 16.9 %all-to-all-start.2 = ((bf16[8,9,2048]{2,1,0:T(8,128)(2,1)}), bf16[8,9,2048]{2,1,0:T(8,128)(2,1)S(1)}, u32[]{:S(2)}, u32[]{:S(2)}) async-start(bf16[8,9,2048]{2,1,0:T(8,128)(2,1)} %reshape.266), calls=%async_computation.2 | async-start | bytes 1048576 | tf_op jit(solution)/shard_map/while/body/eval_jaxpr/all_to_all | solution.py:134
  440.2 18.8 %all-to-all-start.1 = ((bf16[8,9,2048]{2,1,0:T(8,128)(2,1)}), bf16[8,9,2048]{2,1,0:T(8,128)(2,1)S(1)}, u32[]{:S(2)}, u32[]{:S(2)}) async-start(bf16[8,9,2048]{2,1,0:T(8,128)(2,1)} %reshape.265), calls=%async_computation.1 | async-start | bytes 1048576 | tf_op jit(solution)/shard_map/while/body/eval_jaxpr/all_to_all | solution.py:120
  459.1 18.3 %all-to-all-start = ((bf16[8,9,2048]{2,1,0:T(8,128)(2,1)}), bf16[8,9,2048]{2,1,0:T(8,128)(2,1)S(1)}, u32[]{:S(2)}, u32[]{:S(2)}) async-start(bf16[8,9,2048]{2,1,0:T(8,128)(2,1)} %reshape.263), calls=%async_computation | async-start | bytes 1048576 | tf_op jit(solution)/shard_map/while/body/eval_jaxpr/all_to_all | solution.py:121
  502.3 16.9 %all-to-all-start.2 = ((bf16[8,9,2048]{2,1,0:T(8,128)(2,1)}), bf16[8,9,2048]{2,1,0:T(8,128)(2,1)S(1)}, u32[]{:S(2)}, u32[]{:S(2)}) async-start(bf16[8,9,2048]{2,1,0:T(8,128)(2,1)} %reshape.266), calls=%async_computation.2 | async-start | bytes 1048576 | tf_op jit(solution)/shard_map/while/body/eval_jaxpr/all_to_all | solution.py:134
  528.4 18.8 %all-to-all-start.1 = ((bf16[8,9,2048]{2,1,0:T(8,128)(2,1)}), bf16[8,9,2048]{2,1,0:T(8,128)(2,1)S(1)}, u32[]{:S(2)}, u32[]{:S(2)}) async-start(bf16[8,9,2048]{2,1,0:T(8,128)(2,1)} %reshape.265), calls=%async_computation.1 | async-start | bytes 1048576 | tf_op jit(solution)/shard_map/while/body/eval_jaxpr/all_to_all | solution.py:120
  547.2 18.3 %all-to-all-start = ((bf16[8,9,2048]{2,1,0:T(8,128)(2,1)}), bf16[8,9,2048]{2,1,0:T(8,128)(2,1)S(1)}, u32[]{:S(2)}, u32[]{:S(2)}) async-start(bf16[8,9,2048]{2,1,0:T(8,128)(2,1)} %reshape.263), calls=%async_computation | async-start | bytes 1048576 | tf_op jit(solution)/shard_map/while/body/eval_jaxpr/all_to_all | solution.py:121
  590.5 16.9 %all-to-all-start.2 = ((bf16[8,9,2048]{2,1,0:T(8,128)(2,1)}), bf16[8,9,2048]{2,1,0:T(8,128)(2,1)S(1)}, u32[]{:S(2)}, u32[]{:S(2)}) async-start(bf16[8,9,2048]{2,1,0:T(8,128)(2,1)} %reshape.266), calls=%async_computation.2 | async-start | bytes 1048576 | tf_op jit(solution)/shard_map/while/body/eval_jaxpr/all_to_all | solution.py:134
  616.5 18.8 %all-to-all-start.1 = ((bf16[8,9,2048]{2,1,0:T(8,128)(2,1)}), bf16[8,9,2048]{2,1,0:T(8,128)(2,1)S(1)}, u32[]{:S(2)}, u32[]{:S(2)}) async-start(bf16[8,9,2048]{2,1,0:T(8,128)(2,1)} %reshape.265), calls=%async_computation.1 | async-start | bytes 1048576 | tf_op jit(solution)/shard_map/while/body/eval_jaxpr/all_to_all | solution.py:120
  635.4 18.3 %all-to-all-start = ((bf16[8,9,2048]{2,1,0:T(8,128)(2,1)}), bf16[8,9,2048]{2,1,0:T(8,128)(2,1)S(1)}, u32[]{:S(2)}, u32[]{:S(2)}) async-start(bf16[8,9,2048]{2,1,0:T(8,128)(2,1)} %reshape.263), calls=%async_computation | async-start | bytes 1048576 | tf_op jit(solution)/shard_map/while/body/eval_jaxpr/all_to_all | solution.py:121
  678.7 16.9 %all-to-all-start.2 = ((bf16[8,9,2048]{2,1,0:T(8,128)(2,1)}), bf16[8,9,2048]{2,1,0:T(8,128)(2,1)S(1)}, u32[]{:S(2)}, u32[]{:S(2)}) async-start(bf16[8,9,2048]{2,1,0:T(8,128)(2,1)} %reshape.266), calls=%async_computation.2 | async-start | bytes 1048576 | tf_op jit(solution)/shard_map/while/body/eval_jaxpr/all_to_all | solution.py:134
  704.7 18.8 %all-to-all-start.1 = ((bf16[8,9,2048]{2,1,0:T(8,128)(2,1)}), bf16[8,9,2048]{2,1,0:T(8,128)(2,1)S(1)}, u32[]{:S(2)}, u32[]{:S(2)}) async-start(bf16[8,9,2048]{2,1,0:T(8,128)(2,1)} %reshape.265), calls=%async_computation.1 | async-start | bytes 1048576 | tf_op jit(solution)/shard_map/while/body/eval_jaxpr/all_to_all | solution.py:120
  723.6 18.3 %all-to-all-start = ((bf16[8,9,2048]{2,1,0:T(8,128)(2,1)}), bf16[8,9,2048]{2,1,0:T(8,128)(2,1)S(1)}, u32[]{:S(2)}, u32[]{:S(2)}) async-start(bf16[8,9,2048]{2,1,0:T(8,128)(2,1)} %reshape.263), calls=%async_computation | async-start | bytes 1048576 | tf_op jit(solution)/shard_map/while/body/eval_jaxpr/all_to_all | solution.py:121
  789.6 18.8 %all-to-all-start.1 = ((bf16[8,9,2048]{2,1,0:T(8,128)(2,1)}), bf16[8,9,2048]{2,1,0:T(8,128)(2,1)S(1)}, u32[]{:S(2)}, u32[]{:S(2)}) async-start(bf16[8,9,2048]{2,1,0:T(8,128)(2,1)} %reshape.265), calls=%async_computation.1 | async-start | bytes 1048576 | tf_op jit(solution)/shard_map/while/body/eval_jaxpr/all_to_all | solution.py:120
  808.5 18.3 %all-to-all-start = ((bf16[8,9,2048]{2,1,0:T(8,128)(2,1)}), bf16[8,9,2048]{2,1,0:T(8,128)(2,1)S(1)}, u32[]{:S(2)}, u32[]{:S(2)}) async-start(bf16[8,9,2048]{2,1,0:T(8,128)(2,1)} %reshape.263), calls=%async_computation | async-start | bytes 1048576 | tf_op jit(solution)/shard_map/while/body/eval_jaxpr/all_to_all | solution.py:121
  837.7 16.9 %all-to-all-start.2 = ((bf16[8,9,2048]{2,1,0:T(8,128)(2,1)}), bf16[8,9,2048]{2,1,0:T(8,128)(2,1)S(1)}, u32[]{:S(2)}, u32[]{:S(2)}) async-start(bf16[8,9,2048]{2,1,0:T(8,128)(2,1)} %reshape.266), calls=%async_computation.2 | async-start | bytes 1048576 | tf_op jit(solution)/shard_map/while/body/eval_jaxpr/all_to_all | solution.py:134
  863.7 18.8 %all-to-all-start.1 = ((bf16[8,9,2048]{2,1,0:T(8,128)(2,1)}), bf16[8,9,2048]{2,1,0:T(8,128)(2,1)S(1)}, u32[]{:S(2)}, u32[]{:S(2)}) async-start(bf16[8,9,2048]{2,1,0:T(8,128)(2,1)} %reshape.265), calls=%async_computation.1 | async-start | bytes 1048576 | tf_op jit(solution)/shard_map/while/body/eval_jaxpr/all_to_all | solution.py:120
  882.6 18.3 %all-to-all-start = ((bf16[8,9,2048]{2,1,0:T(8,128)(2,1)}), bf16[8,9,2048]{2,1,0:T(8,128)(2,1)S(1)}, u32[]{:S(2)}, u32[]{:S(2)}) async-start(bf16[8,9,2048]{2,1,0:T(8,128)(2,1)} %reshape.263), calls=%async_computation | async-start | bytes 1048576 | tf_op jit(solution)/shard_map/while/body/eval_jaxpr/all_to_all | solution.py:121
  911.7 16.9 %all-to-all-start.2 = ((bf16[8,9,2048]{2,1,0:T(8,128)(2,1)}), bf16[8,9,2048]{2,1,0:T(8,128)(2,1)S(1)}, u32[]{:S(2)}, u32[]{:S(2)}) async-start(bf16[8,9,2048]{2,1,0:T(8,128)(2,1)} %reshape.266), calls=%async_computation.2 | async-start | bytes 1048576 | tf_op jit(solution)/shard_map/while/body/eval_jaxpr/all_to_all | solution.py:134
  (59 other events, 670.3 us)
where the time goes:
time: 939 us; the launch traced here: 932 us
  waiting for transfers between devices  498 us (53%)
  starting transfers between devices  189 us (20%)
  matrix products  138 us (15%)
  local copies, waits for them, and re-layouts  60.3 us (6%)
  other arithmetic  37.8 us (4%)
    all_to_all x11, waiting for transfers between devices, advance(): lax.all_to_all(sent_grad, 'expert', split_axis=0, concat_axis=0, tiled=True)  155 us
    all_to_all x11, waiting for transfers between devices, advance(): lax.all_to_all(sent_normed, 'expert', split_axis=0, concat_axis=0, tiled=...  144 us
    all_to_all x11, waiting for transfers between devices, advance(): lax.all_to_all(returned.reshape(experts, capacity, width), 'expert', spli...  139 us
    all_to_all x11, waiting for transfers between devices, advance(): lax.all_to_all(dprob.reshape(experts, capacity).astype(jnp.bfloat16), 'ex...  58.5 us
    all_to_all x11, starting transfers between devices, advance(): lax.all_to_all(sent_normed, 'expert', split_axis=0, concat_axis=0, tiled=...  43.6 us
    all_to_all x11, starting transfers between devices, advance(): lax.all_to_all(dprob.reshape(experts, capacity).astype(jnp.bfloat16), 'ex...  42.3 us
    all_to_all x11, starting transfers between devices, advance(): lax.all_to_all(sent_grad, 'expert', split_axis=0, concat_axis=0, tiled=True)  39.9 us
    all_to_all x11, starting transfers between devices, advance(): lax.all_to_all(returned.reshape(experts, capacity, width), 'expert', spli...  38.4 us
  transfers between devices with their start and end apart: 55, of which 45 were waited for; matrix products, arithmetic and copies ran while one was open for 9% of the time, Pallas kernels for 0%

commit v1 on v0

--- a/solution.py
+++ b/solution.py
@@ -2,6 +2,33 @@
 import jax.numpy as jnp
 from jax import lax
 from jax.sharding import PartitionSpec as P
+
+
+def _do_weights(local_array, out_dim, x0):
+    new = local_array.shape
+    then = local_array.reshape(*new[:out_dim], x0, new[out_dim] // x0, *new[out_dim + 1 :])
+    return jnp.moveaxis(then, out_dim, 0)
+
+
+def frame_group(own_rows, pos_dim):
+    own_rows = jnp.moveaxis(own_rows, 0, pos_dim)
+    m_next = own_rows.shape
+    return own_rows.reshape(
+        *m_next[:pos_dim], m_next[pos_dim] * m_next[pos_dim + 1], *m_next[pos_dim + 2 :]
+    )
+
+
+def clear_grid_by_axis(xx, bus_axis, panel, vector=0):
+    y_new, front = (lax.axis_size(bus_axis), lax.axis_index(bus_axis))
+    o_now = _do_weights(xx, panel, y_new)
+    gallery = [o_now[front]]
+    for dev_j in range(1, y_new):
+        carry_in = o_now[(front + dev_j) % y_new]
+        gallery.append(
+            lax.ppermute(carry_in, bus_axis, [(s, (s + dev_j) % y_new) for s in range(y_new)])
+        )
+    o_now = jnp.stack(gallery, 0)[(front - jnp.arange(y_new)) % y_new]
+    return frame_group(o_now, vector)
 
 
 def shifted(shard, axis, by):
@@ -117,7 +144,7 @@
         sent_normed = pack_rows(select, normed, per_token).reshape(experts, capacity, width)
         sent_grad = pack_rows(select, grad_in, per_token).reshape(experts, capacity, width)
         got_normed, got_grad = (
-            lax.all_to_all(sent_normed, "expert", split_axis=0, concat_axis=0, tiled=True),
+            clear_grid_by_axis(sent_normed, "expert", 0),
             lax.all_to_all(sent_grad, "expert", split_axis=0, concat_axis=0, tiled=True),
         )
         rows_normed = got_normed.reshape(slots, width)

time: 939 us -> 886 us (0.944)
  waiting for transfers between devices: 498 us -> 368 us
  starting transfers between devices: 189 us -> 257 us
  local copies, waits for them, and re-layouts: 60.3 us -> 69.8 us
    all_to_all x11 -> x0, waiting for transfers between devices: 144 us -> none  [advance(): lax.all_to_all(sent_normed, 'expert', split_axis=0, concat_axis=0, tiled=...]
    ppermute x0 -> x77, starting transfers between devices: none -> 108 us  [clear_grid_by_axis(): lax.ppermute(carry_in, bus_axis, [(s, (s + dev_j) % y_new) for s in range...]
    all_to_all x11 -> x0, starting transfers between devices: 43.6 us -> none  [advance(): lax.all_to_all(sent_normed, 'expert', split_axis=0, concat_axis=0, tiled=...]
    ppermute x0 -> x77, waiting for transfers between devices: none -> 43.3 us  [clear_grid_by_axis(): lax.ppermute(carry_in, bus_axis, [(s, (s + dev_j) % y_new) for s in range...]
    dot_general x8, matrix products: 25.6 us -> 6.81 us  [expert_rows(): up_rows = jnp.dot(normed_rows, up_w, preferred_element_type=jnp.float32)]
    dot_general x8, matrix products: 7.72 us -> 26.2 us  [expert_rows(): output = jnp.dot(hidden, down_w, preferred_element_type=jnp.float32)]
    all_to_all x11, waiting for transfers between devices: 155 us -> 138 us  [advance(): lax.all_to_all(sent_grad, 'expert', split_axis=0, concat_axis=0, tiled=True)]
    dot_general x8, matrix products: 28.7 us -> 11.2 us  [expert_rows(): lax.dot_general(grad_rows, down_w, (((1,), (1,)), ((), ())), preferred_el...]
  transfers between devices with their start and end apart: 55 -> 121, of which waited for: 45 -> 54; matrix products, arithmetic and copies ran while one was open for 9% -> 11% of each run, Pallas kernels for 0% -> 0%
where the time goes in v1:
time: 886 us; the launch traced here: 879 us
  waiting for transfers between devices  368 us (42%)
  starting transfers between devices  257 us (29%)
  matrix products  129 us (15%)
  local copies, waits for them, and re-layouts  69.8 us (8%)
  other arithmetic  44.9 us (5%)
    all_to_all x11, waiting for transfers between devices, advance(): lax.all_to_all(sent_grad, 'expert', split_axis=0, concat_axis=0, tiled=True)  138 us
    all_to_all x11, waiting for transfers between devices, advance(): lax.all_to_all(returned.reshape(experts, capacity, width), 'expert', spli...  128 us
    ppermute x77, starting transfers between devices, clear_grid_by_axis(): lax.ppermute(carry_in, bus_axis, [(s, (s + dev_j) % y_new) for s in range...  108 us
    all_to_all x11, waiting for transfers between devices, advance(): lax.all_to_all(dprob.reshape(experts, capacity).astype(jnp.bfloat16), 'ex...  58.5 us
    all_to_all x11, starting transfers between devices, advance(): lax.all_to_all(sent_grad, 'expert', split_axis=0, concat_axis=0, tiled=True)  44.5 us
    ppermute x77, waiting for transfers between devices, clear_grid_by_axis(): lax.ppermute(carry_in, bus_axis, [(s, (s + dev_j) % y_new) for s in range...  43.3 us
    all_to_all x11, starting transfers between devices, advance(): lax.all_to_all(dprob.reshape(experts, capacity).astype(jnp.bfloat16), 'ex...  43.3 us
    all_to_all x11, starting transfers between devices, advance(): lax.all_to_all(returned.reshape(experts, capacity, width), 'expert', spli...  38.4 us
  transfers between devices with their start and end apart: 121, of which 54 were waited for; matrix products, arithmetic and copies ran while one was open for 11% of the time, Pallas kernels for 0%

profile of v1, /device:TPU:2, one launch (start us, length us, event | category | flops | bytes accessed | tf_op | source)
XLA Modules:
  0.0 879.5 jit_solution(1746470085335953606)
XLA Ops:
  10.0 869.5 %while.18 = (s32[]{:T(128)}, bf16[16,2048]{1,0:T(8,128)(2,1)S(1)}, bf16[8,16,2048]{2,1,0:T(8,128)(2,1)}, pred[]{:T(512)}, s32[]{:T(128)}, /*index=5*/bf16[8,16,2...) while((s32[]{:T(128)}, bf16[16,2048]{1,0:T(8,128)(2,1)S(1)}, ...), condition=%wide.region_13.14_spmd.clone, body=%wide.region_0.13_spmd.clone.sunk | while | flops 1876002688 | bytes 112725904 | solution.py:200
  38.1 12.0 %all-to-all-done = bf16[8,9,2048]{2,1,0:T(8,128)(2,1)S(1)} async-done(((bf16[8,9,2048]{2,1,0:T(8,128)(2,1)}), bf16[8,9,2048]{2,1,0:T(8,128)(2,1)S(1)}, u32[]{:S(2)}, u32[]{:S(2)}) %all-to-all-start) | async-done | bytes 294944 | tf_op jit(solution)/shard_map/while/body/eval_jaxpr/all_to_all | solution.py:148
  64.9 9.8 %all-to-all-done.1 = bf16[8,9,2048]{2,1,0:T(8,128)(2,1)S(1)} async-done(((bf16[8,9,2048]{2,1,0:T(8,128)(2,1)}), bf16[8,9,2048]{2,1,0:T(8,128)(2,1)S(1)}, u32[]{:S(2)}, u32[]{:S(2)}) %all-to-all-start.1) | async-done | bytes 294944 | tf_op jit(solution)/shard_map/while/body/eval_jaxpr/all_to_all | solution.py:161
  106.0 11.4 %all-to-all-done = bf16[8,9,2048]{2,1,0:T(8,128)(2,1)S(1)} async-done(((bf16[8,9,2048]{2,1,0:T(8,128)(2,1)}), bf16[8,9,2048]{2,1,0:T(8,128)(2,1)S(1)}, u32[]{:S(2)}, u32[]{:S(2)}) %all-to-all-start) | async-done | bytes 294944 | tf_op jit(solution)/shard_map/while/body/eval_jaxpr/all_to_all | solution.py:148
  117.5 12.9 %conditional.3 = (bf16[72,2048]{1,0:T(8,128)(2,1)S(1)}, bf16[72]{0:T(256)(128)(2,1)S(1)}) conditional(s32[]{:T(128)} %convert_element_type.195, () %tuple.85, (bf16[8,9,2048]{2,1,0:T(8,128)(2,1)S(1)}, bf16[1024,2048]{1,0:T(8,128)(2,1)}, s32[]{:T(128)}, s32[8,1]{0,1:T(1,128)S(1)}, s32[]{:T(128)}, ...), branch_computations={%region_6.6_spmd, %region_7.8_spmd.clone} | conditional | flops 1814299648 | bytes 99651992 | solution.py:159
  131.1 7.2 all-to-all-start.2
  148.7 13.7 %all-to-all-done.1 = bf16[8,9,2048]{2,1,0:T(8,128)(2,1)S(1)} async-done(((bf16[8,9,2048]{2,1,0:T(8,128)(2,1)}), bf16[8,9,2048]{2,1,0:T(8,128)(2,1)S(1)}, u32[]{:S(2)}, u32[]{:S(2)}) %all-to-all-start.1) | async-done | bytes 294944 | tf_op jit(solution)/shard_map/while/body/eval_jaxpr/all_to_all | solution.py:161
  192.6 12.7 %all-to-all-done = bf16[8,9,2048]{2,1,0:T(8,128)(2,1)S(1)} async-done(((bf16[8,9,2048]{2,1,0:T(8,128)(2,1)}), bf16[8,9,2048]{2,1,0:T(8,128)(2,1)S(1)}, u32[]{:S(2)}, u32[]{:S(2)}) %all-to-all-start) | async-done | bytes 294944 | tf_op jit(solution)/shard_map/while/body/eval_jaxpr/all_to_all | solution.py:148
  205.4 12.9 %conditional.3 = (bf16[72,2048]{1,0:T(8,128)(2,1)S(1)}, bf16[72]{0:T(256)(128)(2,1)S(1)}) conditional(s32[]{:T(128)} %convert_element_type.195, () %tuple.85, (bf16[8,9,2048]{2,1,0:T(8,128)(2,1)S(1)}, bf16[1024,2048]{1,0:T(8,128)(2,1)}, s32[]{:T(128)}, s32[8,1]{0,1:T(1,128)S(1)}, s32[]{:T(128)}, ...), branch_computations={%region_6.6_spmd, %region_7.8_spmd.clone} | conditional | flops 1814299648 | bytes 99651992 | solution.py:159
  233.0 11.9 %all-to-all-done.1 = bf16[8,9,2048]{2,1,0:T(8,128)(2,1)S(1)} async-done(((bf16[8,9,2048]{2,1,0:T(8,128)(2,1)}), bf16[8,9,2048]{2,1,0:T(8,128)(2,1)S(1)}, u32[]{:S(2)}, u32[]{:S(2)}) %all-to-all-start.1) | async-done | bytes 294944 | tf_op jit(solution)/shard_map/while/body/eval_jaxpr/all_to_all | solution.py:161
  275.1 12.7 %all-to-all-done = bf16[8,9,2048]{2,1,0:T(8,128)(2,1)S(1)} async-done(((bf16[8,9,2048]{2,1,0:T(8,128)(2,1)}), bf16[8,9,2048]{2,1,0:T(8,128)(2,1)S(1)}, u32[]{:S(2)}, u32[]{:S(2)}) %all-to-all-start) | async-done | bytes 294944 | tf_op jit(solution)/shard_map/while/body/eval_jaxpr/all_to_all | solution.py:148
  287.8 12.9 %conditional.3 = (bf16[72,2048]{1,0:T(8,128)(2,1)S(1)}, bf16[72]{0:T(256)(128)(2,1)S(1)}) conditional(s32[]{:T(128)} %convert_element_type.195, () %tuple.85, (bf16[8,9,2048]{2,1,0:T(8,128)(2,1)S(1)}, bf16[1024,2048]{1,0:T(8,128)(2,1)}, s32[]{:T(128)}, s32[8,1]{0,1:T(1,128)S(1)}, s32[]{:T(128)}, ...), branch_computations={%region_6.6_spmd, %region_7.8_spmd.clone} | conditional | flops 1814299648 | bytes 99651992 | solution.py:159
  315.4 11.9 %all-to-all-done.1 = bf16[8,9,2048]{2,1,0:T(8,128)(2,1)S(1)} async-done(((bf16[8,9,2048]{2,1,0:T(8,128)(2,1)}), bf16[8,9,2048]{2,1,0:T(8,128)(2,1)S(1)}, u32[]{:S(2)}, u32[]{:S(2)}) %all-to-all-start.1) | async-done | bytes 294944 | tf_op jit(solution)/shard_map/while/body/eval_jaxpr/all_to_all | solution.py:161
  357.5 12.7 %all-to-all-done = bf16[8,9,2048]{2,1,0:T(8,128)(2,1)S(1)} async-done(((bf16[8,9,2048]{2,1,0:T(8,128)(2,1)}), bf16[8,9,2048]{2,1,0:T(8,128)(2,1)S(1)}, u32[]{:S(2)}, u32[]{:S(2)}) %all-to-all-start) | async-done | bytes 294944 | tf_op jit(solution)/shard_map/while/body/eval_jaxpr/all_to_all | solution.py:148
  370.2 12.9 %conditional.3 = (bf16[72,2048]{1,0:T(8,128)(2,1)S(1)}, bf16[72]{0:T(256)(128)(2,1)S(1)}) conditional(s32[]{:T(128)} %convert_element_type.195, () %tuple.85, (bf16[8,9,2048]{2,1,0:T(8,128)(2,1)S(1)}, bf16[1024,2048]{1,0:T(8,128)(2,1)}, s32[]{:T(128)}, s32[8,1]{0,1:T(1,128)S(1)}, s32[]{:T(128)}, ...), branch_computations={%region_6.6_spmd, %region_7.8_spmd.clone} | conditional | flops 1814299648 | bytes 99651992 | solution.py:159
  397.8 11.9 %all-to-all-done.1 = bf16[8,9,2048]{2,1,0:T(8,128)(2,1)S(1)} async-done(((bf16[8,9,2048]{2,1,0:T(8,128)(2,1)}), bf16[8,9,2048]{2,1,0:T(8,128)(2,1)S(1)}, u32[]{:S(2)}, u32[]{:S(2)}) %all-to-all-start.1) | async-done | bytes 294944 | tf_op jit(solution)/shard_map/while/body/eval_jaxpr/all_to_all | solution.py:161
  439.9 12.7 %all-to-all-done = bf16[8,9,2048]{2,1,0:T(8,128)(2,1)S(1)} async-done(((bf16[8,9,2048]{2,1,0:T(8,128)(2,1)}), bf16[8,9,2048]{2,1,0:T(8,128)(2,1)S(1)}, u32[]{:S(2)}, u32[]{:S(2)}) %all-to-all-start) | async-done | bytes 294944 | tf_op jit(solution)/shard_map/while/body/eval_jaxpr/all_to_all | solution.py:148
  452.6 12.9 %conditional.3 = (bf16[72,2048]{1,0:T(8,128)(2,1)S(1)}, bf16[72]{0:T(256)(128)(2,1)S(1)}) conditional(s32[]{:T(128)} %convert_element_type.195, () %tuple.85, (bf16[8,9,2048]{2,1,0:T(8,128)(2,1)S(1)}, bf16[1024,2048]{1,0:T(8,128)(2,1)}, s32[]{:T(128)}, s32[8,1]{0,1:T(1,128)S(1)}, s32[]{:T(128)}, ...), branch_computations={%region_6.6_spmd, %region_7.8_spmd.clone} | conditional | flops 1814299648 | bytes 99651992 | solution.py:159
  480.2 11.9 %all-to-all-done.1 = bf16[8,9,2048]{2,1,0:T(8,128)(2,1)S(1)} async-done(((bf16[8,9,2048]{2,1,0:T(8,128)(2,1)}), bf16[8,9,2048]{2,1,0:T(8,128)(2,1)S(1)}, u32[]{:S(2)}, u32[]{:S(2)}) %all-to-all-start.1) | async-done | bytes 294944 | tf_op jit(solution)/shard_map/while/body/eval_jaxpr/all_to_all | solution.py:161
  522.3 12.7 %all-to-all-done = bf16[8,9,2048]{2,1,0:T(8,128)(2,1)S(1)} async-done(((bf16[8,9,2048]{2,1,0:T(8,128)(2,1)}), bf16[8,9,2048]{2,1,0:T(8,128)(2,1)S(1)}, u32[]{:S(2)}, u32[]{:S(2)}) %all-to-all-start) | async-done | bytes 294944 | tf_op jit(solution)/shard_map/while/body/eval_jaxpr/all_to_all | solution.py:148
  535.0 12.9 %conditional.3 = (bf16[72,2048]{1,0:T(8,128)(2,1)S(1)}, bf16[72]{0:T(256)(128)(2,1)S(1)}) conditional(s32[]{:T(128)} %convert_element_type.195, () %tuple.85, (bf16[8,9,2048]{2,1,0:T(8,128)(2,1)S(1)}, bf16[1024,2048]{1,0:T(8,128)(2,1)}, s32[]{:T(128)}, s32[8,1]{0,1:T(1,128)S(1)}, s32[]{:T(128)}, ...), branch_computations={%region_6.6_spmd, %region_7.8_spmd.clone} | conditional | flops 1814299648 | bytes 99651992 | solution.py:159
  562.6 11.9 %all-to-all-done.1 = bf16[8,9,2048]{2,1,0:T(8,128)(2,1)S(1)} async-done(((bf16[8,9,2048]{2,1,0:T(8,128)(2,1)}), bf16[8,9,2048]{2,1,0:T(8,128)(2,1)S(1)}, u32[]{:S(2)}, u32[]{:S(2)}) %all-to-all-start.1) | async-done | bytes 294944 | tf_op jit(solution)/shard_map/while/body/eval_jaxpr/all_to_all | solution.py:161
  604.7 12.7 %all-to-all-done = bf16[8,9,2048]{2,1,0:T(8,128)(2,1)S(1)} async-done(((bf16[8,9,2048]{2,1,0:T(8,128)(2,1)}), bf16[8,9,2048]{2,1,0:T(8,128)(2,1)S(1)}, u32[]{:S(2)}, u32[]{:S(2)}) %all-to-all-start) | async-done | bytes 294944 | tf_op jit(solution)/shard_map/while/body/eval_jaxpr/all_to_all | solution.py:148
  617.4 12.9 %conditional.3 = (bf16[72,2048]{1,0:T(8,128)(2,1)S(1)}, bf16[72]{0:T(256)(128)(2,1)S(1)}) conditional(s32[]{:T(128)} %convert_element_type.195, () %tuple.85, (bf16[8,9,2048]{2,1,0:T(8,128)(2,1)S(1)}, bf16[1024,2048]{1,0:T(8,128)(2,1)}, s32[]{:T(128)}, s32[8,1]{0,1:T(1,128)S(1)}, s32[]{:T(128)}, ...), branch_computations={%region_6.6_spmd, %region_7.8_spmd.clone} | conditional | flops 1814299648 | bytes 99651992 | solution.py:159
  645.0 11.9 %all-to-all-done.1 = bf16[8,9,2048]{2,1,0:T(8,128)(2,1)S(1)} async-done(((bf16[8,9,2048]{2,1,0:T(8,128)(2,1)}), bf16[8,9,2048]{2,1,0:T(8,128)(2,1)S(1)}, u32[]{:S(2)}, u32[]{:S(2)}) %all-to-all-start.1) | async-done | bytes 294944 | tf_op jit(solution)/shard_map/while/body/eval_jaxpr/all_to_all | solution.py:161
  687.1 12.7 %all-to-all-done = bf16[8,9,2048]{2,1,0:T(8,128)(2,1)S(1)} async-done(((bf16[8,9,2048]{2,1,0:T(8,128)(2,1)}), bf16[8,9,2048]{2,1,0:T(8,128)(2,1)S(1)}, u32[]{:S(2)}, u32[]{:S(2)}) %all-to-all-start) | async-done | bytes 294944 | tf_op jit(solution)/shard_map/while/body/eval_jaxpr/all_to_all | solution.py:148
  699.8 12.9 %conditional.3 = (bf16[72,2048]{1,0:T(8,128)(2,1)S(1)}, bf16[72]{0:T(256)(128)(2,1)S(1)}) conditional(s32[]{:T(128)} %convert_element_type.195, () %tuple.85, (bf16[8,9,2048]{2,1,0:T(8,128)(2,1)S(1)}, bf16[1024,2048]{1,0:T(8,128)(2,1)}, s32[]{:T(128)}, s32[8,1]{0,1:T(1,128)S(1)}, s32[]{:T(128)}, ...), branch_computations={%region_6.6_spmd, %region_7.8_spmd.clone} | conditional | flops 1814299648 | bytes 99651992 | solution.py:159
  727.4 9.8 %all-to-all-done.1 = bf16[8,9,2048]{2,1,0:T(8,128)(2,1)S(1)} async-done(((bf16[8,9,2048]{2,1,0:T(8,128)(2,1)}), bf16[8,9,2048]{2,1,0:T(8,128)(2,1)S(1)}, u32[]{:S(2)}, u32[]{:S(2)}) %all-to-all-start.1) | async-done | bytes 294944 | tf_op jit(solution)/shard_map/while/body/eval_jaxpr/all_to_all | solution.py:161
  767.4 12.7 %all-to-all-done = bf16[8,9,2048]{2,1,0:T(8,128)(2,1)S(1)} async-done(((bf16[8,9,2048]{2,1,0:T(8,128)(2,1)}), bf16[8,9,2048]{2,1,0:T(8,128)(2,1)S(1)}, u32[]{:S(2)}, u32[]{:S(2)}) %all-to-all-start) | async-done | bytes 294944 | tf_op jit(solution)/shard_map/while/body/eval_jaxpr/all_to_all | solution.py:148
  794.8 11.8 %all-to-all-done.1 = bf16[8,9,2048]{2,1,0:T(8,128)(2,1)S(1)} async-done(((bf16[8,9,2048]{2,1,0:T(8,128)(2,1)}), bf16[8,9,2048]{2,1,0:T(8,128)(2,1)S(1)}, u32[]{:S(2)}, u32[]{:S(2)}) %all-to-all-start.1) | async-done | bytes 294944 | tf_op jit(solution)/shard_map/while/body/eval_jaxpr/all_to_all | solution.py:161
  836.9 12.7 %all-to-all-done = bf16[8,9,2048]{2,1,0:T(8,128)(2,1)S(1)} async-done(((bf16[8,9,2048]{2,1,0:T(8,128)(2,1)}), bf16[8,9,2048]{2,1,0:T(8,128)(2,1)S(1)}, u32[]{:S(2)}, u32[]{:S(2)}) %all-to-all-start) | async-done | bytes 294944 | tf_op jit(solution)/shard_map/while/body/eval_jaxpr/all_to_all | solution.py:148
  864.3 11.9 %all-to-all-done.1 = bf16[8,9,2048]{2,1,0:T(8,128)(2,1)S(1)} async-done(((bf16[8,9,2048]{2,1,0:T(8,128)(2,1)}), bf16[8,9,2048]{2,1,0:T(8,128)(2,1)S(1)}, u32[]{:S(2)}, u32[]{:S(2)}) %all-to-all-start.1) | async-done | bytes 294944 | tf_op jit(solution)/shard_map/while/body/eval_jaxpr/all_to_all | solution.py:161
  (924 shorter events, 601.8 us)
Async XLA Ops:
  10.0 22.3 %collective-permute-start = (bf16[16,2048]{1,0:T(8,128)(2,1)S(1)}, bf16[16,2048]{1,0:T(8,128)(2,1)S(1)}, u32[]{:S(2)}, u32[]{:S(2)}) collective-permute-start(bf16[16,2048]{1,0:T(8,128)(2,1)S(1)} %broadcast_select_fusion.2), channel_id=1, source_target_pairs={{8,0},{16,8},{24,16},{9,1},{17,9},{25,17},{10,2},{18,10},{26,18},{... | collective-permute-start | bytes 196616 | tf_op jit(solution)/shard_map/while/body/eval_jaxpr/ppermute | solution.py:37
  33.7 16.4 %all-to-all-start = ((bf16[8,9,2048]{2,1,0:T(8,128)(2,1)}), bf16[8,9,2048]{2,1,0:T(8,128)(2,1)S(1)}, u32[]{:S(2)}, u32[]{:S(2)}) async-start(bf16[8,9,2048]{2,1,0:T(8,128)(2,1)} %reshape.303), calls=%async_computation | async-start | bytes 1048576 | tf_op jit(solution)/shard_map/while/body/eval_jaxpr/all_to_all | solution.py:148
  61.0 13.7 %all-to-all-start.1 = ((bf16[8,9,2048]{2,1,0:T(8,128)(2,1)}), bf16[8,9,2048]{2,1,0:T(8,128)(2,1)S(1)}, u32[]{:S(2)}, u32[]{:S(2)}) async-start(bf16[8,9,2048]{2,1,0:T(8,128)(2,1)} %reshape.306), calls=%async_computation.1 | async-start | bytes 1048576 | tf_op jit(solution)/shard_map/while/body/eval_jaxpr/all_to_all | solution.py:161
  78.0 21.5 %collective-permute-start = (bf16[16,2048]{1,0:T(8,128)(2,1)S(1)}, bf16[16,2048]{1,0:T(8,128)(2,1)S(1)}, u32[]{:S(2)}, u32[]{:S(2)}) collective-permute-start(bf16[16,2048]{1,0:T(8,128)(2,1)S(1)} %broadcast_select_fusion.2), channel_id=1, source_target_pairs={{8,0},{16,8},{24,16},{9,1},{17,9},{25,17},{10,2},{18,10},{26,18},{... | collective-permute-start | bytes 196616 | tf_op jit(solution)/shard_map/while/body/eval_jaxpr/ppermute | solution.py:37
  101.0 16.5 %all-to-all-start = ((bf16[8,9,2048]{2,1,0:T(8,128)(2,1)}), bf16[8,9,2048]{2,1,0:T(8,128)(2,1)S(1)}, u32[]{:S(2)}, u32[]{:S(2)}) async-start(bf16[8,9,2048]{2,1,0:T(8,128)(2,1)} %reshape.303), calls=%async_computation | async-start | bytes 1048576 | tf_op jit(solution)/shard_map/while/body/eval_jaxpr/all_to_all | solution.py:148
  144.8 17.6 %all-to-all-start.1 = ((bf16[8,9,2048]{2,1,0:T(8,128)(2,1)}), bf16[8,9,2048]{2,1,0:T(8,128)(2,1)S(1)}, u32[]{:S(2)}, u32[]{:S(2)}) async-start(bf16[8,9,2048]{2,1,0:T(8,128)(2,1)} %reshape.306), calls=%async_computation.1 | async-start | bytes 1048576 | tf_op jit(solution)/shard_map/while/body/eval_jaxpr/all_to_all | solution.py:161
  165.7 21.5 %collective-permute-start = (bf16[16,2048]{1,0:T(8,128)(2,1)S(1)}, bf16[16,2048]{1,0:T(8,128)(2,1)S(1)}, u32[]{:S(2)}, u32[]{:S(2)}) collective-permute-start(bf16[16,2048]{1,0:T(8,128)(2,1)S(1)} %broadcast_select_fusion.2), channel_id=1, source_target_pairs={{8,0},{16,8},{24,16},{9,1},{17,9},{25,17},{10,2},{18,10},{26,18},{... | collective-permute-start | bytes 196616 | tf_op jit(solution)/shard_map/while/body/eval_jaxpr/ppermute | solution.py:37
  188.7 16.6 %all-to-all-start = ((bf16[8,9,2048]{2,1,0:T(8,128)(2,1)}), bf16[8,9,2048]{2,1,0:T(8,128)(2,1)S(1)}, u32[]{:S(2)}, u32[]{:S(2)}) async-start(bf16[8,9,2048]{2,1,0:T(8,128)(2,1)} %reshape.303), calls=%async_computation | async-start | bytes 1048576 | tf_op jit(solution)/shard_map/while/body/eval_jaxpr/all_to_all | solution.py:148
  229.1 15.8 %all-to-all-start.1 = ((bf16[8,9,2048]{2,1,0:T(8,128)(2,1)}), bf16[8,9,2048]{2,1,0:T(8,128)(2,1)S(1)}, u32[]{:S(2)}, u32[]{:S(2)}) async-start(bf16[8,9,2048]{2,1,0:T(8,128)(2,1)} %reshape.306), calls=%async_computation.1 | async-start | bytes 1048576 | tf_op jit(solution)/shard_map/while/body/eval_jaxpr/all_to_all | solution.py:161
  248.1 21.5 %collective-permute-start = (bf16[16,2048]{1,0:T(8,128)(2,1)S(1)}, bf16[16,2048]{1,0:T(8,128)(2,1)S(1)}, u32[]{:S(2)}, u32[]{:S(2)}) collective-permute-start(bf16[16,2048]{1,0:T(8,128)(2,1)S(1)} %broadcast_select_fusion.2), channel_id=1, source_target_pairs={{8,0},{16,8},{24,16},{9,1},{17,9},{25,17},{10,2},{18,10},{26,18},{... | collective-permute-start | bytes 196616 | tf_op jit(solution)/shard_map/while/body/eval_jaxpr/ppermute | solution.py:37
  271.1 16.6 %all-to-all-start = ((bf16[8,9,2048]{2,1,0:T(8,128)(2,1)}), bf16[8,9,2048]{2,1,0:T(8,128)(2,1)S(1)}, u32[]{:S(2)}, u32[]{:S(2)}) async-start(bf16[8,9,2048]{2,1,0:T(8,128)(2,1)} %reshape.303), calls=%async_computation | async-start | bytes 1048576 | tf_op jit(solution)/shard_map/while/body/eval_jaxpr/all_to_all | solution.py:148
  311.5 15.8 %all-to-all-start.1 = ((bf16[8,9,2048]{2,1,0:T(8,128)(2,1)}), bf16[8,9,2048]{2,1,0:T(8,128)(2,1)S(1)}, u32[]{:S(2)}, u32[]{:S(2)}) async-start(bf16[8,9,2048]{2,1,0:T(8,128)(2,1)} %reshape.306), calls=%async_computation.1 | async-start | bytes 1048576 | tf_op jit(solution)/shard_map/while/body/eval_jaxpr/all_to_all | solution.py:161
  330.5 21.5 %collective-permute-start = (bf16[16,2048]{1,0:T(8,128)(2,1)S(1)}, bf16[16,2048]{1,0:T(8,128)(2,1)S(1)}, u32[]{:S(2)}, u32[]{:S(2)}) collective-permute-start(bf16[16,2048]{1,0:T(8,128)(2,1)S(1)} %broadcast_select_fusion.2), channel_id=1, source_target_pairs={{8,0},{16,8},{24,16},{9,1},{17,9},{25,17},{10,2},{18,10},{26,18},{... | collective-permute-start | bytes 196616 | tf_op jit(solution)/shard_map/while/body/eval_jaxpr/ppermute | solution.py:37
  353.5 16.6 %all-to-all-start = ((bf16[8,9,2048]{2,1,0:T(8,128)(2,1)}), bf16[8,9,2048]{2,1,0:T(8,128)(2,1)S(1)}, u32[]{:S(2)}, u32[]{:S(2)}) async-start(bf16[8,9,2048]{2,1,0:T(8,128)(2,1)} %reshape.303), calls=%async_computation | async-start | bytes 1048576 | tf_op jit(solution)/shard_map/while/body/eval_jaxpr/all_to_all | solution.py:148
  393.9 15.8 %all-to-all-start.1 = ((bf16[8,9,2048]{2,1,0:T(8,128)(2,1)}), bf16[8,9,2048]{2,1,0:T(8,128)(2,1)S(1)}, u32[]{:S(2)}, u32[]{:S(2)}) async-start(bf16[8,9,2048]{2,1,0:T(8,128)(2,1)} %reshape.306), calls=%async_computation.1 | async-start | bytes 1048576 | tf_op jit(solution)/shard_map/while/body/eval_jaxpr/all_to_all | solution.py:161
  412.9 21.5 %collective-permute-start = (bf16[16,2048]{1,0:T(8,128)(2,1)S(1)}, bf16[16,2048]{1,0:T(8,128)(2,1)S(1)}, u32[]{:S(2)}, u32[]{:S(2)}) collective-permute-start(bf16[16,2048]{1,0:T(8,128)(2,1)S(1)} %broadcast_select_fusion.2), channel_id=1, source_target_pairs={{8,0},{16,8},{24,16},{9,1},{17,9},{25,17},{10,2},{18,10},{26,18},{... | collective-permute-start | bytes 196616 | tf_op jit(solution)/shard_map/while/body/eval_jaxpr/ppermute | solution.py:37
  435.9 16.6 %all-to-all-start = ((bf16[8,9,2048]{2,1,0:T(8,128)(2,1)}), bf16[8,9,2048]{2,1,0:T(8,128)(2,1)S(1)}, u32[]{:S(2)}, u32[]{:S(2)}) async-start(bf16[8,9,2048]{2,1,0:T(8,128)(2,1)} %reshape.303), calls=%async_computation | async-start | bytes 1048576 | tf_op jit(solution)/shard_map/while/body/eval_jaxpr/all_to_all | solution.py:148
  476.3 15.8 %all-to-all-start.1 = ((bf16[8,9,2048]{2,1,0:T(8,128)(2,1)}), bf16[8,9,2048]{2,1,0:T(8,128)(2,1)S(1)}, u32[]{:S(2)}, u32[]{:S(2)}) async-start(bf16[8,9,2048]{2,1,0:T(8,128)(2,1)} %reshape.306), calls=%async_computation.1 | async-start | bytes 1048576 | tf_op jit(solution)/shard_map/while/body/eval_jaxpr/all_to_all | solution.py:161
  495.3 21.5 %collective-permute-start = (bf16[16,2048]{1,0:T(8,128)(2,1)S(1)}, bf16[16,2048]{1,0:T(8,128)(2,1)S(1)}, u32[]{:S(2)}, u32[]{:S(2)}) collective-permute-start(bf16[16,2048]{1,0:T(8,128)(2,1)S(1)} %broadcast_select_fusion.2), channel_id=1, source_target_pairs={{8,0},{16,8},{24,16},{9,1},{17,9},{25,17},{10,2},{18,10},{26,18},{... | collective-permute-start | bytes 196616 | tf_op jit(solution)/shard_map/while/body/eval_jaxpr/ppermute | solution.py:37
  518.3 16.6 %all-to-all-start = ((bf16[8,9,2048]{2,1,0:T(8,128)(2,1)}), bf16[8,9,2048]{2,1,0:T(8,128)(2,1)S(1)}, u32[]{:S(2)}, u32[]{:S(2)}) async-start(bf16[8,9,2048]{2,1,0:T(8,128)(2,1)} %reshape.303), calls=%async_computation | async-start | bytes 1048576 | tf_op jit(solution)/shard_map/while/body/eval_jaxpr/all_to_all | solution.py:148
  558.7 15.8 %all-to-all-start.1 = ((bf16[8,9,2048]{2,1,0:T(8,128)(2,1)}), bf16[8,9,2048]{2,1,0:T(8,128)(2,1)S(1)}, u32[]{:S(2)}, u32[]{:S(2)}) async-start(bf16[8,9,2048]{2,1,0:T(8,128)(2,1)} %reshape.306), calls=%async_computation.1 | async-start | bytes 1048576 | tf_op jit(solution)/shard_map/while/body/eval_jaxpr/all_to_all | solution.py:161
  577.7 21.5 %collective-permute-start = (bf16[16,2048]{1,0:T(8,128)(2,1)S(1)}, bf16[16,2048]{1,0:T(8,128)(2,1)S(1)}, u32[]{:S(2)}, u32[]{:S(2)}) collective-permute-start(bf16[16,2048]{1,0:T(8,128)(2,1)S(1)} %broadcast_select_fusion.2), channel_id=1, source_target_pairs={{8,0},{16,8},{24,16},{9,1},{17,9},{25,17},{10,2},{18,10},{26,18},{... | collective-permute-start | bytes 196616 | tf_op jit(solution)/shard_map/while/body/eval_jaxpr/ppermute | solution.py:37
  600.7 16.6 %all-to-all-start = ((bf16[8,9,2048]{2,1,0:T(8,128)(2,1)}), bf16[8,9,2048]{2,1,0:T(8,128)(2,1)S(1)}, u32[]{:S(2)}, u32[]{:S(2)}) async-start(bf16[8,9,2048]{2,1,0:T(8,128)(2,1)} %reshape.303), calls=%async_computation | async-start | bytes 1048576 | tf_op jit(solution)/shard_map/while/body/eval_jaxpr/all_to_all | solution.py:148
  641.1 15.8 %all-to-all-start.1 = ((bf16[8,9,2048]{2,1,0:T(8,128)(2,1)}), bf16[8,9,2048]{2,1,0:T(8,128)(2,1)S(1)}, u32[]{:S(2)}, u32[]{:S(2)}) async-start(bf16[8,9,2048]{2,1,0:T(8,128)(2,1)} %reshape.306), calls=%async_computation.1 | async-start | bytes 1048576 | tf_op jit(solution)/shard_map/while/body/eval_jaxpr/all_to_all | solution.py:161
  660.1 21.5 %collective-permute-start = (bf16[16,2048]{1,0:T(8,128)(2,1)S(1)}, bf16[16,2048]{1,0:T(8,128)(2,1)S(1)}, u32[]{:S(2)}, u32[]{:S(2)}) collective-permute-start(bf16[16,2048]{1,0:T(8,128)(2,1)S(1)} %broadcast_select_fusion.2), channel_id=1, source_target_pairs={{8,0},{16,8},{24,16},{9,1},{17,9},{25,17},{10,2},{18,10},{26,18},{... | collective-permute-start | bytes 196616 | tf_op jit(solution)/shard_map/while/body/eval_jaxpr/ppermute | solution.py:37
  683.1 16.6 %all-to-all-start = ((bf16[8,9,2048]{2,1,0:T(8,128)(2,1)}), bf16[8,9,2048]{2,1,0:T(8,128)(2,1)S(1)}, u32[]{:S(2)}, u32[]{:S(2)}) async-start(bf16[8,9,2048]{2,1,0:T(8,128)(2,1)} %reshape.303), calls=%async_computation | async-start | bytes 1048576 | tf_op jit(solution)/shard_map/while/body/eval_jaxpr/all_to_all | solution.py:148
  740.5 21.5 %collective-permute-start = (bf16[16,2048]{1,0:T(8,128)(2,1)S(1)}, bf16[16,2048]{1,0:T(8,128)(2,1)S(1)}, u32[]{:S(2)}, u32[]{:S(2)}) collective-permute-start(bf16[16,2048]{1,0:T(8,128)(2,1)S(1)} %broadcast_select_fusion.2), channel_id=1, source_target_pairs={{8,0},{16,8},{24,16},{9,1},{17,9},{25,17},{10,2},{18,10},{26,18},{... | collective-permute-start | bytes 196616 | tf_op jit(solution)/shard_map/while/body/eval_jaxpr/ppermute | solution.py:37
  763.5 16.6 %all-to-all-start = ((bf16[8,9,2048]{2,1,0:T(8,128)(2,1)}), bf16[8,9,2048]{2,1,0:T(8,128)(2,1)S(1)}, u32[]{:S(2)}, u32[]{:S(2)}) async-start(bf16[8,9,2048]{2,1,0:T(8,128)(2,1)} %reshape.303), calls=%async_computation | async-start | bytes 1048576 | tf_op jit(solution)/shard_map/while/body/eval_jaxpr/all_to_all | solution.py:148
  790.9 15.8 %all-to-all-start.1 = ((bf16[8,9,2048]{2,1,0:T(8,128)(2,1)}), bf16[8,9,2048]{2,1,0:T(8,128)(2,1)S(1)}, u32[]{:S(2)}, u32[]{:S(2)}) async-start(bf16[8,9,2048]{2,1,0:T(8,128)(2,1)} %reshape.306), calls=%async_computation.1 | async-start | bytes 1048576 | tf_op jit(solution)/shard_map/while/body/eval_jaxpr/all_to_all | solution.py:161
  809.9 21.5 %collective-permute-start = (bf16[16,2048]{1,0:T(8,128)(2,1)S(1)}, bf16[16,2048]{1,0:T(8,128)(2,1)S(1)}, u32[]{:S(2)}, u32[]{:S(2)}) collective-permute-start(bf16[16,2048]{1,0:T(8,128)(2,1)S(1)} %broadcast_select_fusion.2), channel_id=1, source_target_pairs={{8,0},{16,8},{24,16},{9,1},{17,9},{25,17},{10,2},{18,10},{26,18},{... | collective-permute-start | bytes 196616 | tf_op jit(solution)/shard_map/while/body/eval_jaxpr/ppermute | solution.py:37
  832.9 16.6 %all-to-all-start = ((bf16[8,9,2048]{2,1,0:T(8,128)(2,1)}), bf16[8,9,2048]{2,1,0:T(8,128)(2,1)S(1)}, u32[]{:S(2)}, u32[]{:S(2)}) async-start(bf16[8,9,2048]{2,1,0:T(8,128)(2,1)} %reshape.303), calls=%async_computation | async-start | bytes 1048576 | tf_op jit(solution)/shard_map/while/body/eval_jaxpr/all_to_all | solution.py:148
  860.4 15.8 %all-to-all-start.1 = ((bf16[8,9,2048]{2,1,0:T(8,128)(2,1)}), bf16[8,9,2048]{2,1,0:T(8,128)(2,1)S(1)}, u32[]{:S(2)}, u32[]{:S(2)}) async-start(bf16[8,9,2048]{2,1,0:T(8,128)(2,1)} %reshape.306), calls=%async_computation.1 | async-start | bytes 1048576 | tf_op jit(solution)/shard_map/while/body/eval_jaxpr/all_to_all | solution.py:161
  (132 other events, 1351.0 us)
